TPU v7x, 512 devices: a whole 4x4x16 slice. The times are simulated.
512 devices in a mesh: dp: 32 (over z, core), expert: 16 (over x, y).
Axes of the slice: x: 4, y: 4, z: 16, core: 2. Of those that a mesh axis runs over, the one named last changes fastest.
Arguments:
- grad_out: bfloat16 [65536, 2048], P(('dp', 'expert')), may hold values from -6 to 6
- gate: float32 [65536, 1], P(('dp', 'expert')), may hold values from 0.25 to 1
- expert_ids: int32 [65536, 1], P(('dp', 'expert')), may hold values from 0 to 15; in each aligned block of 128 rows (0 to 127, 128 to 255, ...) at most 10 rows name the same one
- w_in: bfloat16 [16, 5120, 2048], P('expert', 'dp'), may hold values from -0.125 to 0.125
- w_out: bfloat16 [16, 5120, 2048], P('expert', 'dp'), may hold values from -0.078125 to 0.078125
- pre_act: bfloat16 [32, 16, 160, 5120], P('dp', 'expert'), may hold values from -6 to 6
Outputs:
- grad_in: bfloat16 [65536, 2048], P(('dp', 'expert'))
Inputs may be any that keep to these rules, and one draw needn't show every extreme that they name: `expert_ids`: among the 128 tokens of one device no expert is named more than 10 times, and in every draw some device names some expert exactly 10 times.
All inputs are finite; a program needn't handle non-finite values.
Results may differ from a plain program's by a relative error of at most 0.0057.
Values may be sent and summed in bfloat16 or wider, within the bound.
No kernel may reach another device: no remote copies, remote signals or barrier semaphores. Data moves between devices by JAX's collectives and lax.ppermute only.
A program may use at most 192 MiB of HBM per device.

v0:
```python
import jax
import jax.numpy as jnp
from jax import lax
from jax.sharding import PartitionSpec as P


def gelu_slope(values):
    inside = 0.7978845608028654 * (values + 0.044715 * values * values * values)
    curved = jnp.tanh(inside)
    return 0.5 * (1.0 + curved) + 0.5 * values * (1.0 - curved * curved) * 0.7978845608028654 * (
        1.0 + 3.0 * 0.044715 * values * values
    )


def body(grad_out, gate, expert_ids, w_in, w_out, pre_act):
    groups = lax.axis_size("expert")
    slots = pre_act.shape[2]
    capacity = slots // groups
    width = grad_out.shape[1]
    chosen = expert_ids[:, 0]
    hit_table = (chosen[:, None] == jnp.arange(groups, dtype=jnp.int32)[None, :]).astype(jnp.int32)
    position = jnp.sum(jnp.cumsum(hit_table, axis=0) * hit_table, axis=1) - 1
    target = chosen * capacity + position
    scaled = (grad_out.astype(jnp.float32) * gate).astype(jnp.bfloat16)
    outgoing = (
        jnp.zeros((slots, width), jnp.bfloat16)
        .at[target]
        .set(scaled)
        .reshape(groups, capacity, width)
    )
    arrived = lax.all_to_all(outgoing, "expert", split_axis=0, concat_axis=0, tiled=True)
    rows_in = arrived.reshape(slots, width)
    stashed = pre_act[0, 0]
    hidden_grad = jnp.einsum(
        "sd,fd->sf",
        rows_in,
        lax.all_gather(w_out, "dp", axis=1, tiled=True)[0],
        preferred_element_type=jnp.float32,
    )
    act_grad = (hidden_grad * gelu_slope(stashed.astype(jnp.float32))).astype(jnp.bfloat16)
    slot_sum = jnp.einsum(
        "sf,fd->sd",
        act_grad,
        lax.all_gather(w_in, "dp", axis=1, tiled=True)[0],
        preferred_element_type=jnp.float32,
    )
    slot_grad = slot_sum.astype(jnp.bfloat16).reshape(groups, capacity, width)
    returned = lax.all_to_all(slot_grad, "expert", split_axis=0, concat_axis=0, tiled=True)
    return returned.reshape(slots, width)[target]


def solution(mesh):
    return jax.shard_map(
        body,
        mesh=mesh,
        in_specs=(
            P(("dp", "expert"), None),
            P(("dp", "expert"), None),
            P(("dp", "expert"), None),
            P("expert", "dp", None),
            P("expert", "dp", None),
            P("dp", "expert", None, None),
        ),
        out_specs=P(("dp", "expert"), None),
        check_vma=False,
    )
```

profile of v0, /device:TPU:8, one launch (start us, length us, event | category | flops | bytes accessed | tf_op | source)
XLA Modules:
  0.0 312.6 jit_solution(17426288469553297094)
XLA Ops:
  6.5 0.0 all-gather.3.cloned.1.call-start
  6.5 0.7 all-gather.3.cloned.1.call-update
  7.3 0.0 all-gather.5.cloned.1.call-start
  7.3 0.7 all-gather.5.cloned.1.call-update
  8.0 0.7 fusion.23
  8.8 0.2 reduce_window_sum.11
  8.9 0.8 select_reduce_fusion
  9.8 0.7 fusion.24
  10.4 2.1 scatter_custom_fusion
  12.5 0.2 reshape.23
  12.8 22.9 %all_to_all.10 = bf16[16,10,2048]{2,1,0:T(8,128)(2,1)S(1)} all-to-all(bf16[16,10,2048]{2,1,0:T(8,128)(2,1)S(1)} %reshape.23), channel_id=1, replica_groups=mesh['dp'=32,'expert'=16] {'expert'}, dimensions={0} | all-to-all | bytes 1310720 | tf_op jit(solution)/shard_map/all_to_all | solution.py:31
  35.7 0.2 reshape.24
  35.9 105.8 %all-gather.3.cloned.1.call-done = bf16[1,5120,2048]{2,1,0:T(8,128)(2,1)} async-done(((bf16[1,160,2048]{2,1,0:T(8,128)(2,1)}), bf16[1,5120,2048]{2,1,0:T(8,128)(2,1)}) %all-gather.3.cloned.1.call-update) | async-done | bytes 20971536 | tf_op jit(solution)/shard_map/all_gather | solution.py:37
  141.7 12.6 %fusion.7 = bf16[160,5120]{1,0:T(8,128)(2,1)S(1)} fusion(bf16[160,2048]{1,0:T(8,128)(2,1)S(1)} %reshape.24, bf16[1,5120,2048]{2,1,0:T(8,128)(2,1)} %all-gather.3.cloned.1.call-done, bf16[1,1,160,5120]{3,2,1,0:T(8,128)(2,1)} %param.11), kind=kOutput, calls=%fused_computation.14 | convolution fusion | flops 3371827200 | bytes 24903680 | tf_op jit(solution)/shard_map/sd,fd->sf/dot_general | solution.py:34
  154.3 115.2 %all-gather.5.cloned.1.call-done = bf16[1,5120,2048]{2,1,0:T(8,128)(2,1)} async-done(((bf16[1,160,2048]{2,1,0:T(8,128)(2,1)}), bf16[1,5120,2048]{2,1,0:T(8,128)(2,1)}) %all-gather.5.cloned.1.call-update) | async-done | bytes 20971536 | tf_op jit(solution)/shard_map/all_gather | solution.py:44
  269.5 9.0 %fusion.17 = bf16[160,2048]{1,0:T(8,128)(2,1)S(1)} fusion(bf16[160,5120]{1,0:T(8,128)(2,1)S(1)} %fusion.7, bf16[1,5120,2048]{2,1,0:T(8,128)(2,1)} %all-gather.5.cloned.1.call-done), kind=kOutput, calls=%fused_computation.22 | convolution fusion | flops 3355770880 | bytes 23265280 | tf_op jit(solution)/shard_map/sf,fd->sd/dot_general | solution.py:41
  278.5 1.2 reshape.25
  279.7 7.3 %all-to-all-start.1 = ((bf16[16,10,2048]{2,1,0:T(8,128)(2,1)}), bf16[16,10,2048]{2,1,0:T(8,128)(2,1)S(1)}, u32[]{:S(2)}, u32[]{:S(2)}) async-start(bf16[16,10,2048]{2,1,0:T(8,128)(2,1)} %reshape.25), calls=%async_computation.1 | async-start | bytes 2097152 | tf_op jit(solution)/shard_map/all_to_all | solution.py:48
  287.0 16.8 %all-to-all-done.1 = bf16[16,10,2048]{2,1,0:T(8,128)(2,1)S(1)} async-done(((bf16[16,10,2048]{2,1,0:T(8,128)(2,1)}), bf16[16,10,2048]{2,1,0:T(8,128)(2,1)S(1)}, u32[]{:S(2)}, u32[]{:S(2)}) %all-to-all-start.1) | async-done | bytes 655392 | tf_op jit(solution)/shard_map/all_to_all | solution.py:48
  303.8 0.2 reshape.26
  304.0 1.7 gather_fusion
  (1 shorter events, 0.0 us)
Async XLA Ops:
  6.5 135.2 %all-gather.3.cloned.1.call-start = ((), (), s32[]{:S(2)}) async-start(), calls=%async_computation.2 | async-start | bytes 21626880 | tf_op jit(solution)/shard_map/all_gather | solution.py:37
  7.3 262.3 %all-gather.5.cloned.1.call-start = ((), (), s32[]{:S(2)}) async-start(), calls=%async_computation.3 | async-start | bytes 21626880 | tf_op jit(solution)/shard_map/all_gather | solution.py:44
  279.7 24.1 %all-to-all-start.1 = ((bf16[16,10,2048]{2,1,0:T(8,128)(2,1)}), bf16[16,10,2048]{2,1,0:T(8,128)(2,1)S(1)}, u32[]{:S(2)}, u32[]{:S(2)}) async-start(bf16[16,10,2048]{2,1,0:T(8,128)(2,1)} %reshape.25), calls=%async_computation.1 | async-start | bytes 2097152 | tf_op jit(solution)/shard_map/all_to_all | solution.py:48
Sparse Core Ops, SparseCore 0:
  9.5 132.2 all-gather.2
  143.8 125.6 all-gather.4
where the time goes:
time: 313 us
  waiting for transfers between devices  239 us (76%)
  blocking collectives  22.9 us (7%)
  matrix products  21.6 us (7%)
  between operations  13.5 us (4%)
  starting transfers between devices  7.29 us (2%)
  other arithmetic  4.53 us (1%)
  local copies, waits for them, and re-layouts  3.59 us (1%)
    all_gather x1, waiting for transfers between devices, body(): lax.all_gather(w_in, 'dp', axis=1, tiled=True)[0]  115 us
    all_gather x1, waiting for transfers between devices, body(): lax.all_gather(w_out, 'dp', axis=1, tiled=True)[0]  106 us
    all_to_all x1, blocking collectives, body(): lax.all_to_all(outgoing, 'expert', split_axis=0, concat_axis=0, tiled=True)  22.9 us
    all_to_all x1, waiting for transfers between devices, body(): lax.all_to_all(slot_grad, 'expert', split_axis=0, concat_axis=0, tiled=True)  16.8 us
    dot_general x1, matrix products, body(): jnp.einsum('sd,fd->sf', rows_in, lax.all_gather(w_out, 'dp', axis=1, tile...  12.6 us
    dot_general x1, matrix products, body(): jnp.einsum('sf,fd->sd', act_grad, lax.all_gather(w_in, 'dp', axis=1, tile...  8.95 us
    all_to_all x1, starting transfers between devices, body(): lax.all_to_all(slot_grad, 'expert', split_axis=0, concat_axis=0, tiled=True)  7.25 us
  transfers between devices with their start and end apart: 3, of which 3 were waited for; matrix products, arithmetic and copies ran while one was open for 6% of the time, Pallas kernels for 0%

commit v1 on v0

--- a/solution.py
+++ b/solution.py
@@ -34,7 +34,12 @@
     hidden_grad = jnp.einsum(
         "sd,fd->sf",
         rows_in,
-        lax.all_gather(w_out, "dp", axis=1, tiled=True)[0],
+        jnp.concatenate(
+            lax.all_to_all(
+                jnp.stack([w_out for _ in range(lax.axis_size("dp"))], axis=0), "dp", 0, 0
+            ),
+            axis=1,
+        )[0],
         preferred_element_type=jnp.float32,
     )
     act_grad = (hidden_grad * gelu_slope(stashed.astype(jnp.float32))).astype(jnp.bfloat16)

time: 313 us -> 1130 us (3.61)
  the two profiles are of different devices: /device:TPU:8 before, /device:TPU:32 now
where the time goes in v1:
time: 1130 us
  waiting for transfers between devices  1030 us (91%)
  matrix products  24.4 us (2%)
  blocking collectives  23.7 us (2%)
  starting transfers between devices  19.4 us (2%)
  between operations  13.5 us (1%)
    all_to_all x1, waiting for transfers between devices, body(): lax.all_to_all(jnp.stack([w_out for _ in range(lax.axis_size('dp'))], axi...  1010 us
    all_to_all x1, blocking collectives, body(): lax.all_to_all(outgoing, 'expert', split_axis=0, concat_axis=0, tiled=True)  23.7 us
  transfers between devices with their start and end apart: 3, of which 2 were waited for; matrix products, arithmetic and copies ran while one was open for 1% of the time, Pallas kernels for 0%

profile of v1, /device:TPU:32, one launch (start us, length us, event | category | flops | bytes accessed | tf_op | source)
XLA Modules:
  0.0 1127.0 jit_solution(9865189509837379109)
XLA Ops:
  6.5 0.0 copy-start
  6.5 0.8 fusion.16
  7.3 0.2 reduce_window_sum.11
  7.5 0.8 select_reduce_fusion
  8.3 0.7 fusion.17
  9.0 2.1 scatter_custom_fusion
  11.1 0.2 reshape.26
  11.4 23.7 %all_to_all.15 = bf16[16,10,2048]{2,1,0:T(8,128)(2,1)S(1)} all-to-all(bf16[16,10,2048]{2,1,0:T(8,128)(2,1)S(1)} %reshape.26), channel_id=1, replica_groups=mesh['dp'=32,'expert'=16] {'expert'}, dimensions={0} | all-to-all | bytes 1310720 | tf_op jit(solution)/shard_map/all_to_all | solution.py:31
  35.0 0.0 copy-done
  35.0 7.4 stack.2
  42.5 0.0 copy-start.1
  42.5 15.5 %all-to-all-start.1 = ((bf16[32,1,160,2048]{3,2,1,0:T(8,128)(2,1)}), bf16[32,1,160,2048]{3,2,1,0:T(8,128)(2,1)}, u32[]{:S(2)}, u32[]{:S(2)}) async-start(bf16[32,1,160,2048]{3,2,1,0:T(8,128)(2,1)} %stack.2), calls=%async_computation.1 | async-start | bytes 41943040 | tf_op jit(solution)/shard_map/all_to_all | solution.py:38
  58.0 0.0 all-gather.2.cloned.1.call-start
  58.0 0.7 all-gather.2.cloned.1.call-update
  58.7 0.2 reshape.27
  59.0 1012.5 %all-to-all-done.1 = bf16[32,1,160,2048]{3,2,1,0:T(8,128)(2,1)} async-done(((bf16[32,1,160,2048]{3,2,1,0:T(8,128)(2,1)}), bf16[32,1,160,2048]{3,2,1,0:T(8,128)(2,1)}, u32[]{:S(2)}, u32[]{:S(2)}) %all-to-all-start.1) | async-done | bytes 20971552 | tf_op jit(solution)/shard_map/all_to_all | solution.py:38
  1071.5 0.0 copy-done.1
  1071.5 13.4 %fusion.2 = bf16[160,5120]{1,0:T(8,128)(2,1)} fusion(bf16[160,2048]{1,0:T(8,128)(2,1)S(1)} %reshape.27, bf16[5120,2048]{1,0:T(8,128)(2,1)} %bitcast.5, bf16[1,1,160,5120]{3,2,1,0:T(8,128)(2,1)S(1)} %copy-done.1), kind=kOutput, calls=%fused_computation.12 | convolution fusion | flops 3371827200 | bytes 24903680 | tf_op jit(solution)/shard_map/sd,fd->sf/dot_general | solution.py:34
  1084.9 0.0 all-gather.2.cloned.1.call-done
  1084.9 11.0 fusion.10
  1095.9 1.2 reshape.28
  1097.1 3.8 all-to-all-start.2
  1100.9 17.2 %all-to-all-done.2 = bf16[16,10,2048]{2,1,0:T(8,128)(2,1)S(1)} async-done(((bf16[16,10,2048]{2,1,0:T(8,128)(2,1)}), bf16[16,10,2048]{2,1,0:T(8,128)(2,1)S(1)}, u32[]{:S(2)}, u32[]{:S(2)}) %all-to-all-start.2) | async-done | bytes 655392 | tf_op jit(solution)/shard_map/all_to_all | solution.py:53
  1118.2 0.2 reshape.29
  1118.4 1.7 gather_fusion
  (1 shorter events, 0.0 us)
Async XLA Ops:
  6.5 28.5 %copy-start = (bf16[1,160,2048]{2,1,0:T(8,128)(2,1)S(1)}, bf16[1,160,2048]{2,1,0:T(8,128)(2,1)}, u32[]{:S(2)}) copy-start(bf16[1,160,2048]{2,1,0:T(8,128)(2,1)} %param.10) | copy-start | bytes 1966084
  42.5 1029.0 %copy-start.1 = (bf16[1,1,160,5120]{3,2,1,0:T(8,128)(2,1)S(1)}, bf16[1,1,160,5120]{3,2,1,0:T(8,128)(2,1)}, u32[]{:S(2)}) copy-start(bf16[1,1,160,5120]{3,2,1,0:T(8,128)(2,1)} %param.11) | copy-start | bytes 4915204
  42.5 1029.0 %all-to-all-start.1 = ((bf16[32,1,160,2048]{3,2,1,0:T(8,128)(2,1)}), bf16[32,1,160,2048]{3,2,1,0:T(8,128)(2,1)}, u32[]{:S(2)}, u32[]{:S(2)}) async-start(bf16[32,1,160,2048]{3,2,1,0:T(8,128)(2,1)} %stack.2), calls=%async_computation.1 | async-start | bytes 41943040 | tf_op jit(solution)/shard_map/all_to_all | solution.py:38
  58.0 1026.9 %all-gather.2.cloned.1.call-start = ((), (), s32[]{:S(2)}) async-start(), calls=%async_computation.3 | async-start | bytes 21626880 | tf_op jit(solution)/shard_map/all_gather | solution.py:49
  1097.1 21.1 %all-to-all-start.2 = ((bf16[16,10,2048]{2,1,0:T(8,128)(2,1)}), bf16[16,10,2048]{2,1,0:T(8,128)(2,1)S(1)}, u32[]{:S(2)}, u32[]{:S(2)}) async-start(bf16[16,10,2048]{2,1,0:T(8,128)(2,1)} %reshape.28), calls=%async_computation.2 | async-start | bytes 2097152 | tf_op jit(solution)/shard_map/all_to_all | solution.py:53
Sparse Core Ops, SparseCore 0:
  60.9 581.1 all-gather.1
